TPU v7x, 32 devices: a whole 2x2x4 slice. The times are simulated.
32 devices in a mesh: rep: 2 (over y), grp: 4 (over z), sub: 4 (over x, core).
Axes of the slice: x: 2, y: 2, z: 4, core: 2. Of those that a mesh axis runs over, the one named last changes fastest.
Arguments:
- volume: bfloat16 [256, 8, 8, 128], P(None, ('rep', 'grp'), 'sub'), parts along dimension 1, may hold values from -6 to 6
- cotangent: bfloat16 [256, 8, 8, 128], P(None, ('rep', 'grp'), 'sub'), parts along dimension 1, may hold values from -6 to 6
- first_weight: bfloat16 [256, 256], replicated, may hold values from -0.375 to 0.375
- group_weight: bfloat16 [256, 8, 3, 3, 3], replicated, may hold values from -0.4375 to 0.4375
- third_weight: bfloat16 [256, 256], replicated, may hold values from -0.375 to 0.375
Outputs:
- block_output: bfloat16 [256, 8, 8, 128], P(None, ('rep', 'grp'), 'sub'), parts along dimension 1
- volume_grad: bfloat16 [256, 8, 8, 128], P(None, ('rep', 'grp'), 'sub'), parts along dimension 1
- first_grad: float32 [512, 256], P('rep'), parts along dimension 0
- group_grad: float32 [512, 8, 3, 3, 3], P(('rep', 'grp')), parts along dimension 0
- third_grad: float32 [512, 256], P('rep'), parts along dimension 0
There are 2 independent parts, one for each index of `rep`. A program takes and returns all parts, laid end to end along the dimension named above; an argument that names none is the same for every part. Nothing has to cross between parts.
All inputs are finite; a program needn't handle non-finite values.
Results may differ from a plain program's by a relative error of at most 0.0073.
Values may be sent and summed in bfloat16 or wider, within the bound.
No kernel may reach another device: no remote copies, remote signals or barrier semaphores. Data moves between devices by JAX's collectives and lax.ppermute only.
A program may use at most 64 MiB of HBM per device.

v0:
```python
import math
import jax
import jax.numpy as jnp
from jax import lax
from jax.sharding import PartitionSpec as P

GW = 8


def padded_2(block, sides, width):
    for axis, dim in sides:
        count = lax.axis_size(axis)
        forward = [(i, i + 1) for i in range(count - 1)]
        backward = [(target, source) for source, target in forward]
        low = lax.ppermute(
            lax.slice_in_dim(block, block.shape[dim] - width, None, axis=dim), axis, forward
        )
        high = lax.ppermute(lax.slice_in_dim(block, 0, width, axis=dim), axis, backward)
        block = jnp.concatenate([low, block, high], axis=dim)
    return block


def silu_slope(values):
    sigma = jax.nn.sigmoid(values)
    return sigma * (1.0 + values * (1.0 - sigma))


def dense_conv(source, kernel, depth_pad):
    padding = ((depth_pad, depth_pad), (0, 0), (1, 1))
    return lax.conv_general_dilated(
        source[None],
        kernel,
        (1, 1, 1),
        padding,
        dimension_numbers=("NCDHW", "OIDHW", "NCDHW"),
        preferred_element_type=jnp.float32,
    )[0]


def block_diagonal(kernel):
    rows = kernel.shape[0]
    tiled = jnp.tile(kernel, (1, rows // GW, 1, 1, 1))
    group_of = jnp.arange(rows) // GW
    mask = (group_of[:, None] == group_of[None, :]).astype(kernel.dtype)
    return tiled * mask[:, :, None, None, None]


def diagonal_blocks(dense):
    rows = dense.shape[1]
    groups = rows // GW
    shaped = dense.reshape(groups, GW, rows, *dense.shape[2:])
    group_of = jnp.arange(rows) // GW
    mask = (jnp.arange(groups)[:, None] == group_of[None, :]).astype(dense.dtype)
    picked = (shaped * mask[:, None, :, None, None, None]).sum(axis=0)
    return picked.transpose(1, 0, 2, 3, 4)


def weight_grad(padded, deltas):
    return lax.conv_general_dilated(
        padded[None],
        deltas[None],
        (1, 1, 1),
        "VALID",
        dimension_numbers=("CNDHW", "IODHW", "NCDHW"),
        preferred_element_type=jnp.float32,
    )


def per_device(volume, cotangent, first_weight, group_weight, third_weight):
    channels, depth, height, width = volume.shape
    flattened = volume.reshape(channels, -1)
    contract_lead = (((0,), (0,)), ((), ()))
    contract_tail = (((1,), (1,)), ((), ()))
    total_cells = depth * lax.axis_size("grp") * height * lax.axis_size("sub") * width
    factor = 1.0 / math.sqrt(total_cells)
    group_rows = channels // lax.axis_size("grp")
    first_pre = lax.dot_general(
        first_weight, flattened, contract_lead, preferred_element_type=jnp.float32
    )
    first_act = jax.nn.silu(first_pre).astype(jnp.bfloat16).reshape(volume.shape)
    own_kernel = lax.dynamic_slice_in_dim(
        group_weight, lax.axis_index("grp") * group_rows, group_rows, 0
    )
    dense_kernel = block_diagonal(own_kernel)
    gathered = lax.all_to_all(first_act, "grp", split_axis=0, concat_axis=1, tiled=True)
    padded_act = padded_2(gathered, (("sub", 2),), 1)
    group_pre = dense_conv(padded_act, dense_kernel, 1)
    group_act = jax.nn.silu(group_pre).astype(jnp.bfloat16)
    returned = lax.all_to_all(group_act, "grp", split_axis=1, concat_axis=0, tiled=True)
    act_flat = returned.reshape(channels, -1)
    summed = flattened.astype(jnp.float32) + lax.dot_general(
        third_weight, act_flat, contract_lead, preferred_element_type=jnp.float32
    )
    block_output = jax.nn.silu(summed).astype(jnp.bfloat16).reshape(volume.shape)
    third_delta = (cotangent.reshape(channels, -1).astype(jnp.float32) * silu_slope(summed)).astype(
        jnp.bfloat16
    )
    third_part = lax.dot_general(
        act_flat, third_delta, contract_tail, preferred_element_type=jnp.float32
    )
    third_grad = lax.psum(third_part, ("grp", "sub")) * factor
    hidden_grad = (
        jnp.dot(third_weight, third_delta, preferred_element_type=jnp.float32)
        .astype(jnp.bfloat16)
        .reshape(volume.shape)
    )
    arriving = lax.all_to_all(hidden_grad, "grp", split_axis=0, concat_axis=1, tiled=True)
    group_delta = (arriving.astype(jnp.float32) * silu_slope(group_pre)).astype(jnp.bfloat16)
    delta_rim = padded_2(group_delta, (("sub", 2),), 1)
    flipped = dense_kernel.transpose(1, 0, 2, 3, 4)[:, :, ::-1, ::-1, ::-1]
    inner_local = dense_conv(delta_rim, flipped, 1).astype(jnp.bfloat16)
    dense_grad = weight_grad(jnp.pad(padded_act, ((0, 0), (1, 1), (0, 0), (1, 1))), group_delta)
    kernel_part = diagonal_blocks(dense_grad)
    inner_grad = lax.all_to_all(inner_local, "grp", split_axis=1, concat_axis=0, tiled=True)
    group_grad = lax.psum(kernel_part, "sub") * factor
    first_delta = (
        inner_grad.reshape(channels, -1).astype(jnp.float32) * silu_slope(first_pre)
    ).astype(jnp.bfloat16)
    first_part = lax.dot_general(
        flattened, first_delta, contract_tail, preferred_element_type=jnp.float32
    )
    volume_grad = (
        (
            third_delta.astype(jnp.float32)
            + jnp.dot(first_weight, first_delta, preferred_element_type=jnp.float32)
        )
        .astype(jnp.bfloat16)
        .reshape(volume.shape)
    )
    first_grad = lax.psum(first_part, ("grp", "sub")) * factor
    return (block_output, volume_grad, first_grad, group_grad, third_grad)


def solution(mesh):
    in_specs = (
        P(None, ("rep", "grp"), "sub", None),
        P(None, ("rep", "grp"), "sub", None),
        P(),
        P(),
        P(),
    )
    out_specs = (
        P(None, ("rep", "grp"), "sub", None),
        P(None, ("rep", "grp"), "sub", None),
        P("rep", None),
        P(("rep", "grp"), None, None, None, None),
        P("rep", None),
    )
    return jax.shard_map(
        per_device, mesh=mesh, in_specs=in_specs, out_specs=out_specs, check_vma=False
    )
```

profile of v0, /device:TPU:1, one launch (start us, length us, event | category | flops | bytes accessed | tf_op | source)
XLA Modules:
  0.0 194.1 jit_solution(14904769792690059259)
XLA Ops:
  7.2 1.0 copy.70
  8.2 1.8 multiply_convert_fusion.2
  10.1 0.8 copy.71
  10.9 5.4 %all-to-all-start = ((bf16[256,1,2,128]{3,2,1,0:T(2,128)(2,1)}), bf16[256,1,2,128]{3,2,1,0:T(2,128)(2,1)S(1)}, u32[]{:S(2)}, u32[]{:S(2)}) async-start(bf16[256,1,2,128]{3,2,1,0:T(2,128)(2,1)} %copy.71), calls=%async_computation | async-start | bytes 262144 | tf_op jit(solution)/shard_map/all_to_all | solution.py:85
  16.4 4.7 %all-to-all-done = bf16[256,1,2,128]{3,2,1,0:T(2,128)(2,1)S(1)} async-done(((bf16[256,1,2,128]{3,2,1,0:T(2,128)(2,1)}), bf16[256,1,2,128]{3,2,1,0:T(2,128)(2,1)S(1)}, u32[]{:S(2)}, u32[]{:S(2)}) %all-to-all-start) | async-done | bytes 131104 | tf_op jit(solution)/shard_map/all_to_all | solution.py:85
  21.1 5.2 %collective-permute-start = (bf16[64,4,1,128]{3,0,1,2:T(8,128)(2,1)S(1)}, bf16[64,4,1,128]{3,0,1,2:T(8,128)(2,1)S(1)}, u32[]{:S(2)}, u32[]{:S(2)}) collective-permute-start(bf16[64,4,1,128]{3,0,1,2:T(8,128)(2,1)S(1)} %get-tuple-element.33), channel_id=1, source_target_pairs={{0,1},{1,2},{2,3},{4,5},{5,6},{6,7},{8,9},{9,10},{10,11},{12,13},{... | collective-permute-start | bytes 196616 | tf_op jit(solution)/shard_map/ppermute | solution.py:15
  26.4 1.9 collective-permute-start.1
  28.4 3.5 %collective-permute-done.1 = bf16[64,4,1,128]{3,0,1,2:T(8,128)(2,1)S(1)} collective-permute-done((bf16[64,4,1,128]{3,0,1,2:T(8,128)(2,1)S(1)}, bf16[64,4,1,128]{3,0,1,2:T(8,128)(2,1)S(1)}, u32[]{:S(2)}, u32[]{:S(2)}) %collective-permute-start.1) | collective-permute-done | bytes 65568 | tf_op jit(solution)/shard_map/ppermute | solution.py:18
  32.0 0.3 copy.107
  32.3 0.3 pad.5.clone
  32.7 0.3 copy-done.5
  33.0 1.2 add_multiply_fusion
  34.2 0.3 copy.76
  34.8 0.7 fusion.28
  35.5 3.3 %all-to-all-start.1 = ((bf16[64,4,2,128]{3,0,2,1:T(8,128)(2,1)}), bf16[64,4,2,128]{3,0,2,1:T(8,128)(2,1)S(1)}, u32[]{:S(2)}, u32[]{:S(2)}) async-start(bf16[64,4,2,128]{3,0,2,1:T(8,128)(2,1)} %fusion.28), calls=%async_computation.1 | async-start | bytes 262144 | tf_op jit(solution)/shard_map/all_to_all | solution.py:89
  38.9 0.8 copy.79
  39.7 0.3 copy.91
  40.2 0.2 pad_bitcast_fusion
  40.5 1.7 copy.93
  42.2 1.4 all-to-all-done.1
  43.7 1.3 fusion.24
  45.2 0.8 copy.80
  46.0 3.3 %all-to-all-start.2 = ((bf16[256,1,2,128]{3,2,1,0:T(2,128)(2,1)}), bf16[256,1,2,128]{3,2,1,0:T(2,128)(2,1)S(1)}, u32[]{:S(2)}, u32[]{:S(2)}) async-start(bf16[256,1,2,128]{3,2,1,0:T(2,128)(2,1)} %copy.80), calls=%async_computation.2 | async-start | bytes 262144 | tf_op jit(solution)/shard_map/all_to_all | solution.py:107
  49.4 0.8 copy.96
  50.1 0.9 fusion.35
  51.1 3.5 %all-to-all-done.2 = bf16[256,1,2,128]{3,2,1,0:T(2,128)(2,1)S(1)} async-done(((bf16[256,1,2,128]{3,2,1,0:T(2,128)(2,1)}), bf16[256,1,2,128]{3,2,1,0:T(2,128)(2,1)S(1)}, u32[]{:S(2)}, u32[]{:S(2)}) %all-to-all-start.2) | async-done | bytes 131104 | tf_op jit(solution)/shard_map/all_to_all | solution.py:107
  54.8 3.7 %collective-permute-start.2 = (bf16[64,4,1,128]{3,0,2,1:T(8,128)(2,1)S(1)}, bf16[64,4,1,128]{3,0,2,1:T(8,128)(2,1)S(1)}, u32[]{:S(2)}, u32[]{:S(2)}) collective-permute-start(bf16[64,4,1,128]{3,0,2,1:T(8,128)(2,1)S(1)} %get-tuple-element.31), channel_id=1, source_target_pairs={{0,1},{1,2},{2,3},{4,5},{5,6},{6,7},{8,9},{9,10},{10,11},{12,13},{... | collective-permute-start | bytes 196616 | tf_op jit(solution)/shard_map/ppermute | solution.py:15
  58.4 1.9 collective-permute-start.3
  60.4 0.4 copy.94
  60.8 3.2 %collective-permute-done.3 = bf16[64,4,1,128]{3,0,2,1:T(8,128)(2,1)S(1)} collective-permute-done((bf16[64,4,1,128]{3,0,2,1:T(8,128)(2,1)S(1)}, bf16[64,4,1,128]{3,0,2,1:T(8,128)(2,1)S(1)}, u32[]{:S(2)}, u32[]{:S(2)}) %collective-permute-start.3) | collective-permute-done | bytes 65568 | tf_op jit(solution)/shard_map/ppermute | solution.py:18
  64.1 0.3 copy.108
  64.4 0.3 pad.7.clone
  64.8 2.1 %fusion.4 = bf16[4,2,8,17,64]{4,2,3,1,0:T(8,128)(2,1)S(1)} fusion(bf16[64,4,4,1,7,2]{0,4,5,2,1,3:T(8,128)(2,1)S(1)} %slice.27, bf16[64,4,4,1,8,17]{0,4,5,2,1,3:T(8,128)(2,1)S(1)} %copy.85, pred[8,17]{0,1:T(8,128)(4,1)S(1)} %copy-done.5, bf16[64,64]{0,1:T(8,128)(2,1)S(1)} %compare_convert_fusion, bf16[64,8,3,3,3]{0,1,4,3,2:T(8,128)(2,1)S(1)} %constant_dynamic-slice_fusion), kind=kOutput, calls=%fused_computation.8 | convolution fusion | flops 202055680 | bytes 482440 | tf_op jit(solution)/shard_map/conv_general_dilated | solution.py:30
  67.3 0.8 copy.87
  68.1 3.3 %all-to-all-start.3 = ((bf16[64,4,2,128]{3,0,2,1:T(8,128)(2,1)}), bf16[64,4,2,128]{3,0,2,1:T(8,128)(2,1)S(1)}, u32[]{:S(2)}, u32[]{:S(2)}) async-start(bf16[64,4,2,128]{3,0,2,1:T(8,128)(2,1)} %copy.87), calls=%async_computation.3 | async-start | bytes 262144 | tf_op jit(solution)/shard_map/all_to_all | solution.py:114
  71.4 0.2 all-reduce.4.cloned.1.call-start
  71.7 7.9 %fusion.3 = f32[8,64,3,3,3]{1,0,4,3,2:T(8,128)S(1)} fusion(bf16[1,64,6,4,130]{1,0,4,3,2:T(2,128)(2,1)S(1)} %copy.93, bf16[1,64,4,2,128]{1,0,4,3,2:T(2,128)(2,1)S(1)} %copy.94, f32[8,64]{1,0:T(8,128)S(1)} %fusion.40), kind=kOutput, calls=%fused_computation.7 | convolution fusion | flops 226699776 | bytes 587776 | tf_op jit(solution)/shard_map/conv_general_dilated | solution.py:59
  79.6 11.5 %psum.22 = f32[64,8,3,3,3]{0,1,4,3,2:T(8,128)S(1)} all-reduce(f32[64,8,3,3,3]{0,1,4,3,2:T(8,128)S(1)} %bitcast.154), channel_id=1, replica_groups=mesh['rep'=2,'grp'=4,'sub'=4] {'sub'}, use_global_device_ids=true, to_apply=%region_2.3 | all-reduce | flops 13824 | bytes 110592 | tf_op jit(solution)/shard_map/psum | solution.py:115
  91.2 0.2 copy.101
  91.4 0.3 reshape.178
  91.9 0.9 convolution_bitcast_fusion.1
  92.9 0.7 broadcast_multiply_fusion.2
  93.5 0.2 fusion.7
  93.7 0.8 copy.97
  94.5 89.9 %all-reduce.4.cloned.1.call-done = (f32[256,256]{0,1:T(8,128)}, f32[256,256]{0,1:T(8,128)}) async-done(((f32[256,256]{0,1:T(8,128)}, f32[256,256]{0,1:T(8,128)}), (f32[256,256]{0,1:T(8,128)}, f32[256,256]{0,1:T(8,128)})) %all-reduce.4.cloned.1.call-update) | async-done | bytes 524304 | tf_op jit(solution)/shard_map/psum | solution.py:130
  184.5 1.1 broadcast_multiply_fusion
  185.5 0.8 copy.98
  186.4 0.8 copy.99
  (41 shorter events, 2.0 us)
Async XLA Ops:
  7.2 36.6 %copy-start = (bf16[256,256]{1,0:T(8,128)(2,1)S(1)}, bf16[256,256]{1,0:T(8,128)(2,1)}, u32[]{:S(2)}) copy-start(bf16[256,256]{1,0:T(8,128)(2,1)} %param.9) | copy-start | bytes 393220
  8.2 20.1 %copy-start.4 = (bf16[256,8,3,3,3]{0,1,4,3,2:T(8,128)(2,1)S(1)}, bf16[256,8,3,3,3]{0,1,4,3,2:T(8,128)(2,1)}, u32[]{:S(2)}) copy-start(bf16[256,8,3,3,3]{0,1,4,3,2:T(8,128)(2,1)} %param.8) | copy-start | bytes 331780
  10.9 10.2 %all-to-all-start = ((bf16[256,1,2,128]{3,2,1,0:T(2,128)(2,1)}), bf16[256,1,2,128]{3,2,1,0:T(2,128)(2,1)S(1)}, u32[]{:S(2)}, u32[]{:S(2)}) async-start(bf16[256,1,2,128]{3,2,1,0:T(2,128)(2,1)} %copy.71), calls=%async_computation | async-start | bytes 262144 | tf_op jit(solution)/shard_map/all_to_all | solution.py:85
  21.1 7.3 %collective-permute-start = (bf16[64,4,1,128]{3,0,1,2:T(8,128)(2,1)S(1)}, bf16[64,4,1,128]{3,0,1,2:T(8,128)(2,1)S(1)}, u32[]{:S(2)}, u32[]{:S(2)}) collective-permute-start(bf16[64,4,1,128]{3,0,1,2:T(8,128)(2,1)S(1)} %get-tuple-element.33), channel_id=1, source_target_pairs={{0,1},{1,2},{2,3},{4,5},{5,6},{6,7},{8,9},{9,10},{10,11},{12,13},{... | collective-permute-start | bytes 196616 | tf_op jit(solution)/shard_map/ppermute | solution.py:15
  26.4 5.6 %collective-permute-start.1 = (bf16[64,4,1,128]{3,0,1,2:T(8,128)(2,1)S(1)}, bf16[64,4,1,128]{3,0,1,2:T(8,128)(2,1)S(1)}, u32[]{:S(2)}, u32[]{:S(2)}) collective-permute-start(bf16[64,4,1,128]{3,0,1,2:T(8,128)(2,1)S(1)} %get-tuple-element.34), channel_id=1, source_target_pairs={{1,0},{2,1},{3,2},{5,4},{6,5},{7,6},{9,8},{10,9},{11,10},{13,12},{... | collective-permute-start | bytes 196616 | tf_op jit(solution)/shard_map/ppermute | solution.py:18
  32.3 0.7 copy-start.5
  34.5 4.3 %copy-start.2 = (bf16[256,1,2,128]{3,2,1,0:T(2,128)(2,1)S(1)}, bf16[256,1,2,128]{3,2,1,0:T(2,128)(2,1)}, u32[]{:S(2)}) copy-start(bf16[256,1,2,128]{3,2,1,0:T(2,128)(2,1)} %param.6) | copy-start | bytes 393220
  35.5 8.1 %all-to-all-start.1 = ((bf16[64,4,2,128]{3,0,2,1:T(8,128)(2,1)}), bf16[64,4,2,128]{3,0,2,1:T(8,128)(2,1)S(1)}, u32[]{:S(2)}, u32[]{:S(2)}) async-start(bf16[64,4,2,128]{3,0,2,1:T(8,128)(2,1)} %fusion.28), calls=%async_computation.1 | async-start | bytes 262144 | tf_op jit(solution)/shard_map/all_to_all | solution.py:89
  46.0 8.6 %all-to-all-start.2 = ((bf16[256,1,2,128]{3,2,1,0:T(2,128)(2,1)}), bf16[256,1,2,128]{3,2,1,0:T(2,128)(2,1)S(1)}, u32[]{:S(2)}, u32[]{:S(2)}) async-start(bf16[256,1,2,128]{3,2,1,0:T(2,128)(2,1)} %copy.80), calls=%async_computation.2 | async-start | bytes 262144 | tf_op jit(solution)/shard_map/all_to_all | solution.py:107
  54.8 6.0 %collective-permute-start.2 = (bf16[64,4,1,128]{3,0,2,1:T(8,128)(2,1)S(1)}, bf16[64,4,1,128]{3,0,2,1:T(8,128)(2,1)S(1)}, u32[]{:S(2)}, u32[]{:S(2)}) collective-permute-start(bf16[64,4,1,128]{3,0,2,1:T(8,128)(2,1)S(1)} %get-tuple-element.31), channel_id=1, source_target_pairs={{0,1},{1,2},{2,3},{4,5},{5,6},{6,7},{8,9},{9,10},{10,11},{12,13},{... | collective-permute-start | bytes 196616 | tf_op jit(solution)/shard_map/ppermute | solution.py:15
  58.4 5.6 %collective-permute-start.3 = (bf16[64,4,1,128]{3,0,2,1:T(8,128)(2,1)S(1)}, bf16[64,4,1,128]{3,0,2,1:T(8,128)(2,1)S(1)}, u32[]{:S(2)}, u32[]{:S(2)}) collective-permute-start(bf16[64,4,1,128]{3,0,2,1:T(8,128)(2,1)S(1)} %get-tuple-element.32), channel_id=1, source_target_pairs={{1,0},{2,1},{3,2},{5,4},{6,5},{7,6},{9,8},{10,9},{11,10},{13,12},{... | collective-permute-start | bytes 196616 | tf_op jit(solution)/shard_map/ppermute | solution.py:18
  68.1 23.1 %all-to-all-start.3 = ((bf16[64,4,2,128]{3,0,2,1:T(8,128)(2,1)}), bf16[64,4,2,128]{3,0,2,1:T(8,128)(2,1)S(1)}, u32[]{:S(2)}, u32[]{:S(2)}) async-start(bf16[64,4,2,128]{3,0,2,1:T(8,128)(2,1)} %copy.87), calls=%async_computation.3 | async-start | bytes 262144 | tf_op jit(solution)/shard_map/all_to_all | solution.py:114
  71.4 113.0 %all-reduce.4.cloned.1.call-start = ((), (), s32[]{:S(2)}) async-start(), calls=%async_computation.4 | async-start | bytes 1048576 | tf_op jit(solution)/shard_map/psum | solution.py:130
  79.6 12.2 %copy-start.1 = (f32[256,256]{0,1:T(8,128)S(1)}, f32[256,256]{0,1:T(8,128)}, u32[]{:S(2)}) copy-start(f32[256,256]{0,1:T(8,128)} %get-tuple-element.36) | copy-start | bytes 786436
  91.4 2.1 %copy-start.3 = (bf16[256,256]{1,0:T(8,128)(2,1)S(1)}, bf16[256,256]{1,0:T(8,128)(2,1)}, u32[]{:S(2)}) copy-start(bf16[256,256]{1,0:T(8,128)(2,1)} %param.7) | copy-start | bytes 393220
Sparse Core Ops, SparseCore 0:
  93.0 91.4 all-reduce.3
where the time goes:
time: 195 us; the launch traced here: 194 us
  waiting for transfers between devices  106 us (54%)
  starting transfers between devices  28.3 us (15%)
  matrix products  16.7 us (9%)
  between operations  14.5 us (7%)
  local copies, waits for them, and re-layouts  13.7 us (7%)
  blocking collectives  11.5 us (6%)
  other arithmetic  2.91 us (1%)
    psum x1, waiting for transfers between devices, per_device(): first_grad = lax.psum(first_part, ('grp', 'sub')) * factor  89.9 us
    psum x1, blocking collectives, per_device(): group_grad = lax.psum(kernel_part, 'sub') * factor  11.5 us
    ppermute x2, starting transfers between devices, padded_2(): lax.ppermute(lax.slice_in_dim(block, block.shape[dim] - width, None, axis...  8.89 us
    conv_general_dilated x1, matrix products, weight_grad(): lax.conv_general_dilated(padded[None], deltas[None], (1, 1, 1), 'VALID',...  7.92 us
    ppermute x2, waiting for transfers between devices, padded_2(): lax.ppermute(lax.slice_in_dim(block, 0, width, axis=dim), axis, backward)  6.74 us
    unnamed x21, local copies, waits for them, and re-layouts  5.57 us
    all_to_all x1, starting transfers between devices, per_device(): lax.all_to_all(first_act, 'grp', split_axis=0, concat_axis=1, tiled=True)  5.42 us
    all_to_all x1, waiting for transfers between devices, per_device(): lax.all_to_all(first_act, 'grp', split_axis=0, concat_axis=1, tiled=True)  4.73 us
  transfers between devices with their start and end apart: 9, of which 6 were waited for; matrix products, arithmetic and copies ran while one was open for 8% of the time, Pallas kernels for 0%

commit v1 on v0

--- a/solution.py
+++ b/solution.py
@@ -127,7 +127,7 @@
         .astype(jnp.bfloat16)
         .reshape(volume.shape)
     )
-    first_grad = lax.psum(first_part, ("grp", "sub")) * factor
+    first_grad = lax.psum(lax.psum(first_part, "sub"), "grp") * factor
     return (block_output, volume_grad, first_grad, group_grad, third_grad)
 
 

time: 195 us -> 242 us (1.24)
  waiting for transfers between devices: 106 us -> 146 us
    psum x1 -> x3, waiting for transfers between devices: 89.9 us -> 129 us  [the longest x1 84.1 us: per_device(): third_grad = lax.psum(third_part, ('grp', 'sub')) * factor]
    all_to_all x1, waiting for transfers between devices: 0.01 us -> 4.24 us  [per_device(): lax.all_to_all(inner_local, 'grp', split_axis=1, concat_axis=0, tiled=True)]
    ppermute x2, waiting for transfers between devices: 6.74 us -> 3.54 us  [padded_2(): lax.ppermute(lax.slice_in_dim(block, 0, width, axis=dim), axis, backward)]
    unnamed x21 -> x19, local copies, waits for them, and re-layouts: 5.57 us -> 5.56 us
  transfers between devices with their start and end apart: 9 -> 11, of which waited for: 6 -> 8; matrix products, arithmetic and copies ran while one was open for 8% -> 7% of each run, Pallas kernels for 0% -> 0%
where the time goes in v1:
time: 242 us; the launch traced here: 239 us
  waiting for transfers between devices  146 us (60%)
  starting transfers between devices  28.4 us (12%)
  matrix products  16.7 us (7%)
  between operations  15.9 us (7%)
  local copies, waits for them, and re-layouts  13.7 us (6%)
  blocking collectives  13.3 us (5%)
  other arithmetic  4.72 us (2%)
    psum x1, waiting for transfers between devices, per_device(): third_grad = lax.psum(third_part, ('grp', 'sub')) * factor  84.1 us
    psum x2, waiting for transfers between devices, per_device(): first_grad = lax.psum(lax.psum(first_part, 'sub'), 'grp') * factor  44.5 us
    psum x1, blocking collectives, per_device(): group_grad = lax.psum(kernel_part, 'sub') * factor  13.3 us
    ppermute x2, starting transfers between devices, padded_2(): lax.ppermute(lax.slice_in_dim(block, block.shape[dim] - width, None, axis...  8.89 us
    conv_general_dilated x1, matrix products, weight_grad(): lax.conv_general_dilated(padded[None], deltas[None], (1, 1, 1), 'VALID',...  7.94 us
    unnamed x19, local copies, waits for them, and re-layouts  5.56 us
    all_to_all x1, starting transfers between devices, per_device(): lax.all_to_all(first_act, 'grp', split_axis=0, concat_axis=1, tiled=True)  5.42 us
  transfers between devices with their start and end apart: 11, of which 8 were waited for; matrix products, arithmetic and copies ran while one was open for 7% of the time, Pallas kernels for 0%

profile of v1, /device:TPU:1, one launch (start us, length us, event | category | flops | bytes accessed | tf_op | source)
XLA Modules:
  0.0 238.8 jit_solution(15135224706127462871)
XLA Ops:
  8.0 1.0 copy.70
  9.1 1.8 multiply_convert_fusion.2
  10.9 0.8 copy.71
  11.7 5.4 %all-to-all-start = ((bf16[256,1,2,128]{3,2,1,0:T(2,128)(2,1)}), bf16[256,1,2,128]{3,2,1,0:T(2,128)(2,1)S(1)}, u32[]{:S(2)}, u32[]{:S(2)}) async-start(bf16[256,1,2,128]{3,2,1,0:T(2,128)(2,1)} %copy.71), calls=%async_computation | async-start | bytes 262144 | tf_op jit(solution)/shard_map/all_to_all | solution.py:85
  17.2 4.7 %all-to-all-done = bf16[256,1,2,128]{3,2,1,0:T(2,128)(2,1)S(1)} async-done(((bf16[256,1,2,128]{3,2,1,0:T(2,128)(2,1)}), bf16[256,1,2,128]{3,2,1,0:T(2,128)(2,1)S(1)}, u32[]{:S(2)}, u32[]{:S(2)}) %all-to-all-start) | async-done | bytes 131104 | tf_op jit(solution)/shard_map/all_to_all | solution.py:85
  22.0 5.2 %collective-permute-start = (bf16[64,4,1,128]{3,0,1,2:T(8,128)(2,1)S(1)}, bf16[64,4,1,128]{3,0,1,2:T(8,128)(2,1)S(1)}, u32[]{:S(2)}, u32[]{:S(2)}) collective-permute-start(bf16[64,4,1,128]{3,0,1,2:T(8,128)(2,1)S(1)} %get-tuple-element.31), channel_id=1, source_target_pairs={{0,1},{1,2},{2,3},{4,5},{5,6},{6,7},{8,9},{9,10},{10,11},{12,13},{... | collective-permute-start | bytes 196616 | tf_op jit(solution)/shard_map/ppermute | solution.py:15
  27.2 1.9 collective-permute-start.1
  29.2 3.5 %collective-permute-done.1 = bf16[64,4,1,128]{3,0,1,2:T(8,128)(2,1)S(1)} collective-permute-done((bf16[64,4,1,128]{3,0,1,2:T(8,128)(2,1)S(1)}, bf16[64,4,1,128]{3,0,1,2:T(8,128)(2,1)S(1)}, u32[]{:S(2)}, u32[]{:S(2)}) %collective-permute-start.1) | collective-permute-done | bytes 65568 | tf_op jit(solution)/shard_map/ppermute | solution.py:18
  32.8 0.3 copy.107
  33.2 0.3 pad.5.clone
  33.6 0.3 copy-done.4
  33.8 1.2 add_multiply_fusion
  35.1 0.3 copy.76
  35.6 0.7 fusion.28
  36.4 3.3 %all-to-all-start.1 = ((bf16[64,4,2,128]{3,0,2,1:T(8,128)(2,1)}), bf16[64,4,2,128]{3,0,2,1:T(8,128)(2,1)S(1)}, u32[]{:S(2)}, u32[]{:S(2)}) async-start(bf16[64,4,2,128]{3,0,2,1:T(8,128)(2,1)} %fusion.28), calls=%async_computation.1 | async-start | bytes 262144 | tf_op jit(solution)/shard_map/all_to_all | solution.py:89
  39.7 0.8 copy.79
  40.5 0.3 copy.91
  41.3 1.7 copy.93
  43.0 1.4 all-to-all-done.1
  44.6 1.3 fusion.24
  46.1 0.8 copy.80
  46.9 3.3 %all-to-all-start.2 = ((bf16[256,1,2,128]{3,2,1,0:T(2,128)(2,1)}), bf16[256,1,2,128]{3,2,1,0:T(2,128)(2,1)S(1)}, u32[]{:S(2)}, u32[]{:S(2)}) async-start(bf16[256,1,2,128]{3,2,1,0:T(2,128)(2,1)} %copy.80), calls=%async_computation.2 | async-start | bytes 262144 | tf_op jit(solution)/shard_map/all_to_all | solution.py:107
  50.2 0.9 fusion.35
  51.2 0.8 copy.96
  52.0 3.5 %all-to-all-done.2 = bf16[256,1,2,128]{3,2,1,0:T(2,128)(2,1)S(1)} async-done(((bf16[256,1,2,128]{3,2,1,0:T(2,128)(2,1)}), bf16[256,1,2,128]{3,2,1,0:T(2,128)(2,1)S(1)}, u32[]{:S(2)}, u32[]{:S(2)}) %all-to-all-start.2) | async-done | bytes 131104 | tf_op jit(solution)/shard_map/all_to_all | solution.py:107
  55.6 3.7 %collective-permute-start.2 = (bf16[64,4,1,128]{3,0,2,1:T(8,128)(2,1)S(1)}, bf16[64,4,1,128]{3,0,2,1:T(8,128)(2,1)S(1)}, u32[]{:S(2)}, u32[]{:S(2)}) collective-permute-start(bf16[64,4,1,128]{3,0,2,1:T(8,128)(2,1)S(1)} %get-tuple-element.29), channel_id=1, source_target_pairs={{0,1},{1,2},{2,3},{4,5},{5,6},{6,7},{8,9},{9,10},{10,11},{12,13},{... | collective-permute-start | bytes 196616 | tf_op jit(solution)/shard_map/ppermute | solution.py:15
  59.3 1.9 collective-permute-start.3
  61.2 84.1 %all-reduce.9.cloned.1.call-done = f32[256,256]{0,1:T(8,128)} async-done(((f32[256,256]{0,1:T(8,128)}), f32[256,256]{0,1:T(8,128)}) %all-reduce.9.cloned.1.call-update) | async-done | bytes 262160 | tf_op jit(solution)/shard_map/psum | solution.py:101
  145.3 1.0 broadcast_multiply_fusion
  146.3 0.8 copy.99
  147.2 0.3 copy.108
  147.5 0.3 pad.7.clone
  147.9 2.1 fusion.4
  150.4 0.8 copy.87
  151.2 3.3 %all-to-all-start.3 = ((bf16[64,4,2,128]{3,0,2,1:T(8,128)(2,1)}), bf16[64,4,2,128]{3,0,2,1:T(8,128)(2,1)S(1)}, u32[]{:S(2)}, u32[]{:S(2)}) async-start(bf16[64,4,2,128]{3,0,2,1:T(8,128)(2,1)} %copy.87), calls=%async_computation.3 | async-start | bytes 262144 | tf_op jit(solution)/shard_map/all_to_all | solution.py:114
  154.6 0.4 copy.94
  155.0 4.2 %all-to-all-done.3 = bf16[64,4,2,128]{3,0,2,1:T(8,128)(2,1)S(1)} async-done(((bf16[64,4,2,128]{3,0,2,1:T(8,128)(2,1)}), bf16[64,4,2,128]{3,0,2,1:T(8,128)(2,1)S(1)}, u32[]{:S(2)}, u32[]{:S(2)}) %all-to-all-start.3) | async-done | bytes 131104 | tf_op jit(solution)/shard_map/all_to_all | solution.py:114
  159.5 0.3 reshape.178
  159.8 1.1 multiply_convert_fusion
  160.9 0.9 convolution_bitcast_fusion.1
  162.1 7.9 %fusion.3 = f32[8,64,3,3,3]{1,0,4,3,2:T(8,128)S(1)} fusion(bf16[1,64,6,4,130]{1,0,4,3,2:T(2,128)(2,1)S(1)} %copy.93, bf16[1,64,4,2,128]{1,0,4,3,2:T(2,128)(2,1)S(1)} %copy.94, f32[8,64]{1,0:T(8,128)S(1)} %fusion.40), kind=kOutput, calls=%fused_computation.7 | convolution fusion | flops 226699776 | bytes 587776 | tf_op jit(solution)/shard_map/conv_general_dilated | solution.py:59
  170.1 13.3 %psum.30 = f32[64,8,3,3,3]{0,1,4,3,2:T(8,128)S(1)} all-reduce(f32[64,8,3,3,3]{0,1,4,3,2:T(8,128)S(1)} %bitcast.154), channel_id=1, replica_groups=mesh['rep'=2,'grp'=4,'sub'=4] {'sub'}, use_global_device_ids=true, to_apply=%region_3.4 | all-reduce | flops 13824 | bytes 110592 | tf_op jit(solution)/shard_map/psum | solution.py:115
  183.3 9.2 %all-reduce.5.cloned.1.call-done = f32[256,256]{0,1:T(8,128)} async-done(((f32[256,256]{0,1:T(8,128)}), f32[256,256]{0,1:T(8,128)}) %all-reduce.5.cloned.1.call-update) | async-done | bytes 262160 | tf_op jit(solution)/shard_map/psum | solution.py:130
  192.5 0.7 broadcast_multiply_fusion.2
  193.4 0.8 copy.97
  194.2 35.3 %all-reduce.7.cloned.1.call-done = f32[256,256]{0,1:T(8,128)} async-done(((f32[256,256]{0,1:T(8,128)}), f32[256,256]{0,1:T(8,128)}) %all-reduce.7.cloned.1.call-update) | async-done | bytes 262160 | tf_op jit(solution)/shard_map/psum | solution.py:130
  229.5 1.0 broadcast_multiply_fusion.1
  230.5 0.8 copy.98
  (46 shorter events, 3.0 us)
Async XLA Ops:
  8.0 36.6 %copy-start = (bf16[256,256]{1,0:T(8,128)(2,1)S(1)}, bf16[256,256]{1,0:T(8,128)(2,1)}, u32[]{:S(2)}) copy-start(bf16[256,256]{1,0:T(8,128)(2,1)} %param.9) | copy-start | bytes 393220
  9.1 20.1 %copy-start.3 = (bf16[256,8,3,3,3]{0,1,4,3,2:T(8,128)(2,1)S(1)}, bf16[256,8,3,3,3]{0,1,4,3,2:T(8,128)(2,1)}, u32[]{:S(2)}) copy-start(bf16[256,8,3,3,3]{0,1,4,3,2:T(8,128)(2,1)} %param.8) | copy-start | bytes 331780
  11.7 10.2 %all-to-all-start = ((bf16[256,1,2,128]{3,2,1,0:T(2,128)(2,1)}), bf16[256,1,2,128]{3,2,1,0:T(2,128)(2,1)S(1)}, u32[]{:S(2)}, u32[]{:S(2)}) async-start(bf16[256,1,2,128]{3,2,1,0:T(2,128)(2,1)} %copy.71), calls=%async_computation | async-start | bytes 262144 | tf_op jit(solution)/shard_map/all_to_all | solution.py:85
  22.0 7.3 %collective-permute-start = (bf16[64,4,1,128]{3,0,1,2:T(8,128)(2,1)S(1)}, bf16[64,4,1,128]{3,0,1,2:T(8,128)(2,1)S(1)}, u32[]{:S(2)}, u32[]{:S(2)}) collective-permute-start(bf16[64,4,1,128]{3,0,1,2:T(8,128)(2,1)S(1)} %get-tuple-element.31), channel_id=1, source_target_pairs={{0,1},{1,2},{2,3},{4,5},{5,6},{6,7},{8,9},{9,10},{10,11},{12,13},{... | collective-permute-start | bytes 196616 | tf_op jit(solution)/shard_map/ppermute | solution.py:15
  27.2 5.6 %collective-permute-start.1 = (bf16[64,4,1,128]{3,0,1,2:T(8,128)(2,1)S(1)}, bf16[64,4,1,128]{3,0,1,2:T(8,128)(2,1)S(1)}, u32[]{:S(2)}, u32[]{:S(2)}) collective-permute-start(bf16[64,4,1,128]{3,0,1,2:T(8,128)(2,1)S(1)} %get-tuple-element.32), channel_id=1, source_target_pairs={{1,0},{2,1},{3,2},{5,4},{6,5},{7,6},{9,8},{10,9},{11,10},{13,12},{... | collective-permute-start | bytes 196616 | tf_op jit(solution)/shard_map/ppermute | solution.py:18
  33.1 0.7 copy-start.4
  35.4 4.3 %copy-start.1 = (bf16[256,1,2,128]{3,2,1,0:T(2,128)(2,1)S(1)}, bf16[256,1,2,128]{3,2,1,0:T(2,128)(2,1)}, u32[]{:S(2)}) copy-start(bf16[256,1,2,128]{3,2,1,0:T(2,128)(2,1)} %param.6) | copy-start | bytes 393220
  36.4 8.1 %all-to-all-start.1 = ((bf16[64,4,2,128]{3,0,2,1:T(8,128)(2,1)}), bf16[64,4,2,128]{3,0,2,1:T(8,128)(2,1)S(1)}, u32[]{:S(2)}, u32[]{:S(2)}) async-start(bf16[64,4,2,128]{3,0,2,1:T(8,128)(2,1)} %fusion.28), calls=%async_computation.1 | async-start | bytes 262144 | tf_op jit(solution)/shard_map/all_to_all | solution.py:89
  46.9 8.6 %all-to-all-start.2 = ((bf16[256,1,2,128]{3,2,1,0:T(2,128)(2,1)}), bf16[256,1,2,128]{3,2,1,0:T(2,128)(2,1)S(1)}, u32[]{:S(2)}, u32[]{:S(2)}) async-start(bf16[256,1,2,128]{3,2,1,0:T(2,128)(2,1)} %copy.80), calls=%async_computation.2 | async-start | bytes 262144 | tf_op jit(solution)/shard_map/all_to_all | solution.py:107
  50.2 95.1 %all-reduce.9.cloned.1.call-start = ((), (), s32[]{:S(2)}) async-start(), calls=%async_computation.6 | async-start | bytes 524288 | tf_op jit(solution)/shard_map/psum | solution.py:101
  55.6 91.5 %collective-permute-start.2 = (bf16[64,4,1,128]{3,0,2,1:T(8,128)(2,1)S(1)}, bf16[64,4,1,128]{3,0,2,1:T(8,128)(2,1)S(1)}, u32[]{:S(2)}, u32[]{:S(2)}) collective-permute-start(bf16[64,4,1,128]{3,0,2,1:T(8,128)(2,1)S(1)} %get-tuple-element.29), channel_id=1, source_target_pairs={{0,1},{1,2},{2,3},{4,5},{5,6},{6,7},{8,9},{9,10},{10,11},{12,13},{... | collective-permute-start | bytes 196616 | tf_op jit(solution)/shard_map/ppermute | solution.py:15
  59.3 87.8 %collective-permute-start.3 = (bf16[64,4,1,128]{3,0,2,1:T(8,128)(2,1)S(1)}, bf16[64,4,1,128]{3,0,2,1:T(8,128)(2,1)S(1)}, u32[]{:S(2)}, u32[]{:S(2)}) collective-permute-start(bf16[64,4,1,128]{3,0,2,1:T(8,128)(2,1)S(1)} %get-tuple-element.30), channel_id=1, source_target_pairs={{1,0},{2,1},{3,2},{5,4},{6,5},{7,6},{9,8},{10,9},{11,10},{13,12},{... | collective-permute-start | bytes 196616 | tf_op jit(solution)/shard_map/ppermute | solution.py:18
  151.2 8.1 %all-to-all-start.3 = ((bf16[64,4,2,128]{3,0,2,1:T(8,128)(2,1)}), bf16[64,4,2,128]{3,0,2,1:T(8,128)(2,1)S(1)}, u32[]{:S(2)}, u32[]{:S(2)}) async-start(bf16[64,4,2,128]{3,0,2,1:T(8,128)(2,1)} %copy.87), calls=%async_computation.3 | async-start | bytes 262144 | tf_op jit(solution)/shard_map/all_to_all | solution.py:114
  154.5 38.0 %all-reduce.5.cloned.1.call-start = ((), (), s32[]{:S(2)}) async-start(), calls=%async_computation.4 | async-start | bytes 524288 | tf_op jit(solution)/shard_map/psum | solution.py:130
  161.9 31.3 %copy-start.2 = (bf16[256,256]{1,0:T(8,128)(2,1)S(1)}, bf16[256,256]{1,0:T(8,128)(2,1)}, u32[]{:S(2)}) copy-start(bf16[256,256]{1,0:T(8,128)(2,1)} %param.7) | copy-start | bytes 393220
  161.9 67.6 %all-reduce.7.cloned.1.call-start = ((), (), s32[]{:S(2)}) async-start(), calls=%async_computation.5 | async-start | bytes 524288 | tf_op jit(solution)/shard_map/psum | solution.py:130
Sparse Core Ops, SparseCore 0:
  55.0 90.2 all-reduce.8
Sparse Core Ops, SparseCore 1:
  161.9 30.5 all-reduce.4
  194.8 34.7 all-reduce.6
